TPU v7x, 128 devices: a whole 4x4x4 slice. The times are simulated.
128 devices in a mesh: req: 8 (over x, core), kv: 16 (over y, z).
Axes of the slice: x: 4, y: 4, z: 4, core: 2. Of those that a mesh axis runs over, the one named last changes fastest.
Arguments:
- x_steps: bfloat16 [4, 1024, 1536], P(None, ('req', 'kv')), may hold values from -6 to 6
- lengths: int32 [128], replicated, may hold values from 16 to 8192
- perm: int32 [128], replicated, may hold values from 0 to 127, as said below
- parents: int32 [4, 1024], replicated, may hold values from 0 to 7
- table: int32 [1024, 9], P(('req', 'kv')), may hold values from 0 to 9215, as said below
- pool: bfloat16 [9216, 128, 256], P(('req', 'kv')), may hold values from -900 to 900
- norm_attn: float32 [1536], replicated, may hold values from 0.1 to 1.9
- w_query: bfloat16 [1536, 1536], replicated, may hold values from -0.15625 to 0.15625
- w_keyval: bfloat16 [1536, 256], replicated, may hold values from -0.15625 to 0.15625
- w_out: bfloat16 [1536, 1536], replicated, may hold values from -0.15625 to 0.15625
- norm_mlp: float32 [1536], replicated, may hold values from 0.1 to 1.9
- w_gate: bfloat16 [1536, 4608], P(None, 'kv'), may hold values from -0.15625 to 0.15625
- w_up: bfloat16 [1536, 4608], P(None, 'kv'), may hold values from -0.15625 to 0.15625
- w_down: bfloat16 [4608, 1536], P('kv'), may hold values from -0.09375 to 0.09375
Outputs:
- outputs: bfloat16 [4, 1024, 1536], P(None, ('req', 'kv'))
Inputs may be any that keep to these rules, and one draw needn't show every extreme that they name: perm is a permutation with perm[s] % 16 == s % 16; among the 8 slots s with one s // 16 and one s % 16 // 8, every req index occurs as perm[s] // 16 exactly once. The entries of row b lie in [(b // 8) * 72, (b // 8 + 1) * 72); no page appears twice in the table.
All inputs are finite; a program needn't handle non-finite values.
Results may differ from a plain program's by a relative error of at most 0.02.
Values may be sent and summed in bfloat16 or wider, within the bound.
No kernel may reach another device: no remote copies, remote signals or barrier semaphores. Data moves between devices by JAX's collectives and lax.ppermute only.
A program may use at most 192 MiB of HBM per device.

v0:
```python
import jax
import jax.numpy as jnp
from jax import lax
from jax.sharding import PartitionSpec as P

WINDOW = 1024
PAGE = 128
BEAMS = 8
EPSILON = 1e-06
NEGATIVE = -1e30


def merged_2(array, axis, combine):
    everything = jax.tree.map(lambda part: lax.all_gather(part, axis), array)
    first = jax.tree.map(lambda part: part[0], everything)

    def turn(k, so_far):
        return combine(so_far, jax.tree.map(lambda part: part[k], everything))

    return lax.fori_loop(1, lax.axis_size(axis), turn, first)


def member_of(beam_index, half_index, halves):
    return beam_index % 2 + 2 * half_index + 2 * halves * (beam_index // 2)


def rms_round(values, gain):
    wide = values.astype(jnp.float32)
    mean_square = jnp.mean(wide * wide, axis=-1, keepdims=True)
    return (wide * lax.rsqrt(mean_square + EPSILON) * gain).astype(jnp.bfloat16)


def page_partial(queries, pages, key_pos, length, step_index):
    head_dim = queries.shape[-1]
    keys = pages[:, :, :head_dim]
    values = pages[:, :, head_dim:]
    scores = jnp.einsum(
        "jrhd,rkd->jrhk", queries, keys, preferred_element_type=jnp.float32
    ) * head_dim ** (-0.5)
    allowed = (key_pos < length[:, None]) & (key_pos > length[:, None] + step_index - WINDOW)
    scores = jnp.where(allowed[None, :, None, :], scores, NEGATIVE)
    highest = jnp.max(scores, axis=-1)
    weights = jnp.exp(scores - highest[..., None]).astype(jnp.bfloat16)
    totals = jnp.sum(weights.astype(jnp.float32), axis=-1)
    weighted = jnp.einsum("jrhk,rkd->jrhd", weights, values, preferred_element_type=jnp.float32)
    return (highest, totals, weighted)


def fresh_partial(queries, entries, count):
    head_dim = queries.shape[-1]
    keys = entries[..., :count, :head_dim]
    values = entries[..., :count, head_dim:]
    scores = jnp.einsum(
        "...hd,...kd->...hk", queries, keys, preferred_element_type=jnp.float32
    ) * head_dim ** (-0.5)
    highest = jnp.max(scores, axis=-1)
    weights = jnp.exp(scores - highest[..., None]).astype(jnp.bfloat16)
    totals = jnp.sum(weights.astype(jnp.float32), axis=-1)
    weighted = jnp.einsum("...hk,...kd->...hd", weights, values, preferred_element_type=jnp.float32)
    return (highest, totals, weighted)


def join_parts(first, second):
    highest = jnp.maximum(first[0], second[0])
    scale_first = jnp.exp(first[0] - highest)
    scale_second = jnp.exp(second[0] - highest)
    totals = first[1] * scale_first + second[1] * scale_second
    weighted = first[2] * scale_first[..., None] + second[2] * scale_second[..., None]
    return (highest, totals, weighted)


def feed_forward(mlp_in, w_gate, w_up, w_down):
    gate = jnp.dot(mlp_in, w_gate, preferred_element_type=jnp.float32)
    upward = jnp.dot(mlp_in, w_up, preferred_element_type=jnp.float32)
    hidden = (jax.nn.gelu(gate, approximate=True) * upward).astype(jnp.bfloat16)
    return jnp.dot(hidden, w_down, preferred_element_type=jnp.float32)


def rank_within(labels, offsets):
    earlier = (labels[None, :] == labels[:, None]) & (offsets[None, :] < offsets[:, None])
    return jnp.sum(earlier.astype(jnp.int32), axis=1)


def pick_half(array, halves, half):
    shaped = array.reshape((BEAMS // 2, halves, 2) + array.shape[1:])
    picked = lax.dynamic_index_in_dim(shaped, half, 1, keepdims=False)
    return picked.reshape((BEAMS,) + array.shape[1:])


def place_block(block, filler, halves, half):
    whole = jnp.full((BEAMS // 2, halves, 2) + block.shape[1:], filler, block.dtype)
    placed = lax.dynamic_update_slice_in_dim(
        whole, block.reshape((BEAMS // 2, 1, 2) + block.shape[1:]), half, 1
    )
    return placed.reshape((BEAMS * halves,) + block.shape[1:])


def on_device(
    x_steps,
    lengths,
    perm,
    parents,
    table,
    pool,
    norm_attn,
    w_query,
    w_keyval,
    w_out,
    norm_mlp,
    w_gate,
    w_up,
    w_down,
):
    steps, rows, width = x_steps.shape
    head_dim = pool.shape[2] // 2
    heads = w_query.shape[1] // head_dim
    span = table.shape[1] * pool.shape[1]
    req_count = lax.axis_size("req")
    kv_count = lax.axis_size("kv")
    group = lax.axis_index("req")
    member = lax.axis_index("kv")
    halves = kv_count // BEAMS
    half = member // 2 % halves
    beam = member % 2 + 2 * (member // (2 * halves))
    per_group = halves * rows
    group_rows = kv_count * rows
    quota = rows // req_count
    offsets = jnp.arange(rows, dtype=jnp.int32)
    slot_ids = group * per_group + half * rows + offsets
    placed = lax.dynamic_slice_in_dim(perm.reshape(req_count, per_group), half * rows, rows, 1)
    serving = lax.dynamic_index_in_dim(placed, group, 0, keepdims=False)
    target = jnp.sum(
        jnp.where(placed == slot_ids[None, :], jnp.arange(req_count, dtype=jnp.int32)[:, None], 0),
        axis=0,
    )
    anchor = serving // per_group
    send_order = jnp.argsort(target * rows + offsets)
    outgoing = x_steps[:, send_order].reshape(steps, req_count, quota, width)
    arrived = lax.all_to_all(outgoing, "req", split_axis=1, concat_axis=1, tiled=True).reshape(
        steps, rows, width
    )
    inputs = arrived[:, anchor * quota + rank_within(anchor, offsets)]
    length = lengths[serving]
    first_page = jnp.maximum(length - WINDOW + 1, 0) // PAGE
    key_pos = first_page[:, None] * PAGE + jnp.arange(span, dtype=jnp.int32)[None, :]
    device = group * kv_count + member
    pages = pool[table - device * pool.shape[0]].reshape(rows, span, 2 * head_dim)
    family = lax.dynamic_slice_in_dim(parents, group * group_rows, group_rows, 1)
    row_ids = jnp.arange(group_rows, dtype=jnp.int32)
    row_member = row_ids // rows
    row_half = row_member // 2 % halves
    within = row_ids % rows
    ancestor = row_member % 2 + 2 * (row_member // (2 * halves))
    recent = jnp.zeros((group_rows, steps, 2 * head_dim), jnp.bfloat16)
    results = []
    for step_index in range(steps):
        parent_rows = member_of(family[step_index], row_half, halves) * rows + within
        ancestor = ancestor[parent_rows]
        recent = recent[parent_rows]
        current = inputs[step_index]
        normed = rms_round(current, norm_attn)
        query = jnp.dot(normed, w_query, preferred_element_type=jnp.float32).astype(jnp.bfloat16)
        fresh = jnp.dot(normed, w_keyval, preferred_element_type=jnp.float32).astype(jnp.bfloat16)
        query_all, fresh_all = (
            lax.all_gather(query, "kv", axis=0, tiled=True),
            lax.all_gather(fresh, "kv", axis=0, tiled=True),
        )
        recent = recent.at[:, step_index].set(fresh_all)
        query_block = pick_half(query_all.reshape(kv_count, rows, heads, head_dim), halves, half)
        held = pick_half(ancestor.reshape(kv_count, rows), halves, half) == beam
        page = page_partial(query_block, pages, key_pos, length, step_index)
        held_heads = held[..., None]
        highest = place_block(jnp.where(held_heads, page[0], NEGATIVE), NEGATIVE, halves, half)
        totals = place_block(jnp.where(held_heads, page[1], 0.0), 0.0, halves, half)
        weighted = place_block(jnp.where(held_heads[..., None], page[2], 0.0), 0.0, halves, half)
        merged = merged_2((highest, totals, weighted), "kv", join_parts)
        page_own = tuple(
            (
                lax.dynamic_index_in_dim(member_part, member, 0, keepdims=False)
                for member_part in merged
            )
        )
        own_entries = lax.dynamic_slice_in_dim(recent, member * rows, rows, 0)
        joined = join_parts(
            page_own,
            fresh_partial(query.reshape(rows, heads, head_dim), own_entries, step_index + 1),
        )
        attended = (
            (joined[2] / joined[1][..., None]).astype(jnp.bfloat16).reshape(rows, heads * head_dim)
        )
        residual = (
            current.astype(jnp.float32)
            + jnp.dot(attended, w_out, preferred_element_type=jnp.float32)
        ).astype(jnp.bfloat16)
        terms = feed_forward(
            lax.all_gather(rms_round(residual, norm_mlp), "kv", axis=0, tiled=True),
            w_gate,
            w_up,
            w_down,
        )
        summed = lax.psum_scatter(
            terms.astype(jnp.bfloat16), "kv", scatter_dimension=0, tiled=True
        ).astype(jnp.float32)
        results.append((residual.astype(jnp.float32) + summed).astype(jnp.bfloat16))
    finished = jnp.stack(results)
    back_order = jnp.argsort(anchor * rows + offsets)
    leaving = finished[:, back_order].reshape(steps, req_count, quota, width)
    returned = lax.all_to_all(leaving, "req", split_axis=1, concat_axis=1, tiled=True).reshape(
        steps, rows, width
    )
    return returned[:, target * quota + rank_within(target, offsets)]


def solution(mesh):
    in_specs = (
        P(None, ("req", "kv"), None),
        P(),
        P(),
        P(),
        P(("req", "kv"), None),
        P(("req", "kv"), None, None),
        P(),
        P(),
        P(),
        P(),
        P(),
        P(None, "kv"),
        P(None, "kv"),
        P("kv", None),
    )
    out_specs = P(None, ("req", "kv"), None)
    return jax.shard_map(
        on_device, mesh=mesh, in_specs=in_specs, out_specs=out_specs, check_vma=False
    )
```

profile of v0, /device:TPU:1, one launch (start us, length us, event | category | flops | bytes accessed | tf_op | source)
XLA Modules:
  0.0 938.8 jit_solution(8522241222401222963)
XLA Ops:
  39.0 20.2 %all_gather.90 = bf16[128,1536]{1,0:T(8,128)(2,1)S(1)} all-gather(bf16[8,1536]{1,0:T(8,128)(2,1)S(1)} %convolution_convert_fusion.4), channel_id=1, replica_groups=mesh['req'=8,'kv'=16] {'kv'}, dimensions={0}, use_global_device_ids=true | all-gather | bytes 417792 | tf_op jit(solution)/shard_map/all_gather | solution.py:165
  67.1 19.5 %all_gather.72 = bf16[128,1536]{1,0:T(8,128)(2,1)S(1)} all-gather(bf16[8,1536]{1,0:T(8,128)(2,1)S(1)} %convolution_convert_fusion.7), channel_id=1, replica_groups=mesh['req'=8,'kv'=16] {'kv'}, dimensions={0}, use_global_device_ids=true | all-gather | bytes 417792 | tf_op jit(solution)/shard_map/all_gather | solution.py:165
  96.3 17.8 %all_gather.78 = bf16[128,1536]{1,0:T(8,128)(2,1)S(1)} all-gather(bf16[8,1536]{1,0:T(8,128)(2,1)S(1)} %convolution_convert_fusion.6), channel_id=1, replica_groups=mesh['req'=8,'kv'=16] {'kv'}, dimensions={0}, use_global_device_ids=true | all-gather | bytes 417792 | tf_op jit(solution)/shard_map/all_gather | solution.py:165
  125.7 20.9 %all_gather.76 = bf16[128,256]{1,0:T(8,128)(2,1)S(1)} all-gather(bf16[8,256]{1,0:T(8,128)(2,1)S(1)} %convolution_convert_fusion.11), channel_id=1, replica_groups=mesh['req'=8,'kv'=16] {'kv'}, dimensions={0}, use_global_device_ids=true | all-gather | bytes 69632 | tf_op jit(solution)/shard_map/all_gather | solution.py:166
  149.5 16.4 %all_gather.82 = bf16[128,256]{1,0:T(8,128)(2,1)S(1)} all-gather(bf16[8,256]{1,0:T(8,128)(2,1)S(1)} %convolution_convert_fusion.10), channel_id=1, replica_groups=mesh['req'=8,'kv'=16] {'kv'}, dimensions={0}, use_global_device_ids=true | all-gather | bytes 69632 | tf_op jit(solution)/shard_map/all_gather | solution.py:166
  168.9 19.8 %all_gather.88 = bf16[128,256]{1,0:T(8,128)(2,1)S(1)} all-gather(bf16[8,256]{1,0:T(8,128)(2,1)S(1)} %convolution_convert_fusion.9), channel_id=1, replica_groups=mesh['req'=8,'kv'=16] {'kv'}, dimensions={0}, use_global_device_ids=true | all-gather | bytes 69632 | tf_op jit(solution)/shard_map/all_gather | solution.py:166
  191.6 16.4 %all_gather.94 = bf16[128,256]{1,0:T(8,128)(2,1)S(1)} all-gather(bf16[8,256]{1,0:T(8,128)(2,1)S(1)} %convolution_convert_fusion.8), channel_id=1, replica_groups=mesh['req'=8,'kv'=16] {'kv'}, dimensions={0}, use_global_device_ids=true | all-gather | bytes 69632 | tf_op jit(solution)/shard_map/all_gather | solution.py:166
  218.9 21.9 %all_gather.84 = bf16[128,1536]{1,0:T(8,128)(2,1)S(1)} all-gather(bf16[8,1536]{1,0:T(8,128)(2,1)S(1)} %convolution_convert_fusion.5), channel_id=1, replica_groups=mesh['req'=8,'kv'=16] {'kv'}, dimensions={0}, use_global_device_ids=true | all-gather | bytes 417792 | tf_op jit(solution)/shard_map/all_gather | solution.py:165
  248.8 20.0 %all_gather.91 = f32[16,16,8,12]{1,2,3,0:T(8,128)} all-gather(f32[1,16,8,12]{1,2,3,0:T(8,128)S(1)} %copy.375), channel_id=1, replica_groups=mesh['req'=8,'kv'=16] {'kv'}, dimensions={0}, use_global_device_ids=true | all-gather | bytes 104448 | tf_op jit(solution)/shard_map/all_gather | solution.py:14
  268.8 22.4 %all_gather.92 = f32[16,16,8,12]{1,2,3,0:T(8,128)} all-gather(f32[1,16,8,12]{1,2,3,0:T(8,128)S(1)} %copy.378), channel_id=1, replica_groups=mesh['req'=8,'kv'=16] {'kv'}, dimensions={0}, use_global_device_ids=true | all-gather | bytes 104448 | tf_op jit(solution)/shard_map/all_gather | solution.py:14
  291.2 20.8 %all_gather.73 = f32[16,16,8,12]{1,2,3,0:T(8,128)S(1)} all-gather(f32[1,16,8,12]{1,2,3,0:T(8,128)S(1)} %copy.320), channel_id=1, replica_groups=mesh['req'=8,'kv'=16] {'kv'}, dimensions={0}, use_global_device_ids=true | all-gather | bytes 104448 | tf_op jit(solution)/shard_map/all_gather | solution.py:14
  312.0 22.6 %all_gather.74 = f32[16,16,8,12]{1,2,3,0:T(8,128)S(1)} all-gather(f32[1,16,8,12]{1,2,3,0:T(8,128)S(1)} %copy.323), channel_id=1, replica_groups=mesh['req'=8,'kv'=16] {'kv'}, dimensions={0}, use_global_device_ids=true | all-gather | bytes 104448 | tf_op jit(solution)/shard_map/all_gather | solution.py:14
  334.6 21.6 %all_gather.79 = f32[16,16,8,12]{1,2,3,0:T(8,128)S(1)} all-gather(f32[1,16,8,12]{1,2,3,0:T(8,128)S(1)} %copy.341), channel_id=1, replica_groups=mesh['req'=8,'kv'=16] {'kv'}, dimensions={0}, use_global_device_ids=true | all-gather | bytes 104448 | tf_op jit(solution)/shard_map/all_gather | solution.py:14
  356.3 18.0 %all_gather.80 = f32[16,16,8,12]{1,2,3,0:T(8,128)S(1)} all-gather(f32[1,16,8,12]{1,2,3,0:T(8,128)S(1)} %copy.344), channel_id=1, replica_groups=mesh['req'=8,'kv'=16] {'kv'}, dimensions={0}, use_global_device_ids=true | all-gather | bytes 104448 | tf_op jit(solution)/shard_map/all_gather | solution.py:14
  374.3 19.4 %all_gather.85 = f32[16,16,8,12]{1,2,3,0:T(8,128)} all-gather(f32[1,16,8,12]{1,2,3,0:T(8,128)S(1)} %copy.358), channel_id=1, replica_groups=mesh['req'=8,'kv'=16] {'kv'}, dimensions={0}, use_global_device_ids=true | all-gather | bytes 104448 | tf_op jit(solution)/shard_map/all_gather | solution.py:14
  393.7 20.4 %all_gather.86 = f32[16,16,8,12]{1,2,3,0:T(8,128)} all-gather(f32[1,16,8,12]{1,2,3,0:T(8,128)S(1)} %copy.361), channel_id=1, replica_groups=mesh['req'=8,'kv'=16] {'kv'}, dimensions={0}, use_global_device_ids=true | all-gather | bytes 104448 | tf_op jit(solution)/shard_map/all_gather | solution.py:14
  426.7 46.2 %while.83 = (s32[]{:T(128)}, f32[16,8,12]{0,1,2:T(8,128)S(1)}, f32[16,8,12]{0,1,2:T(8,128)S(1)}, f32[16,8,12,128]{3,2,1,0:T(8,128)S(1)}, f32[16,16,8,12]{1,2,3,0...) while((s32[]{:T(128)}, f32[16,8,12]{0,1,2:T(8,128)S(1)}, ...), condition=%wide.region_32.33_spmd, body=%wide.region_31.32_spmd.sunk | while | flops 599045 | bytes 4018327 | solution.py:20
  475.2 46.3 %while.80 = (s32[]{:T(128)}, f32[16,8,12]{0,1,2:T(8,128)S(1)}, f32[16,8,12]{0,1,2:T(8,128)S(1)}, f32[16,8,12,128]{3,2,1,0:T(8,128)S(1)}, f32[16,16,8,12]{1,2,3,0...) while((s32[]{:T(128)}, f32[16,8,12]{0,1,2:T(8,128)S(1)}, ...), condition=%wide.region_7.8_spmd, body=%wide.region_6.7_spmd.sunk | while | flops 599045 | bytes 4018327 | solution.py:20
  524.6 73.6 %while.81 = (s32[]{:T(128)}, f32[16,8,12]{0,1,2:T(8,128)S(1)}, f32[16,8,12]{0,1,2:T(8,128)S(1)}, f32[16,8,12,128]{3,2,1,0:T(8,128)}, f32[16,16,8,12]{1,2,3,0:T(8...) while((s32[]{:T(128)}, f32[16,8,12]{0,1,2:T(8,128)S(1)}, ...), condition=%wide.region_14.15_spmd, body=%wide.region_13.14_spmd.sunk | while | flops 599045 | bytes 4018327 | solution.py:20
  610.3 46.2 %while.82 = (s32[]{:T(128)}, f32[16,8,12]{0,1,2:T(8,128)S(1)}, f32[16,8,12]{0,1,2:T(8,128)S(1)}, f32[16,8,12,128]{3,2,1,0:T(8,128)S(1)}, f32[16,16,8,12]{1,2,3,0...) while((s32[]{:T(128)}, f32[16,8,12]{0,1,2:T(8,128)S(1)}, ...), condition=%wide.region_23.24_spmd, body=%wide.region_22.23_spmd.sunk | while | flops 599045 | bytes 4018327 | solution.py:20
  661.8 16.6 %all_gather.95 = bf16[128,1536]{1,0:T(8,128)(2,1)S(1)} all-gather(bf16[8,1536]{1,0:T(8,128)(2,1)S(1)} %get-tuple-element.991), channel_id=1, replica_groups=mesh['req'=8,'kv'=16] {'kv'}, dimensions={0}, use_global_device_ids=true | all-gather | bytes 417792 | tf_op jit(solution)/shard_map/all_gather | solution.py:196
  678.4 17.7 %all_gather.89 = bf16[128,1536]{1,0:T(8,128)(2,1)S(1)} all-gather(bf16[8,1536]{1,0:T(8,128)(2,1)S(1)} %get-tuple-element.990), channel_id=1, replica_groups=mesh['req'=8,'kv'=16] {'kv'}, dimensions={0}, use_global_device_ids=true | all-gather | bytes 417792 | tf_op jit(solution)/shard_map/all_gather | solution.py:196
  722.6 17.9 %all_gather.77 = bf16[128,1536]{1,0:T(8,128)(2,1)S(1)} all-gather(bf16[8,1536]{1,0:T(8,128)(2,1)S(1)} %copy-done.28), channel_id=1, replica_groups=mesh['req'=8,'kv'=16] {'kv'}, dimensions={0}, use_global_device_ids=true | all-gather | bytes 417792 | tf_op jit(solution)/shard_map/all_gather | solution.py:196
  744.1 170.9 %all-reduce.7.cloned.1.call-done = (bf16[128,1536]{1,0:T(8,128)(2,1)}, bf16[128,1536]{1,0:T(8,128)(2,1)}, bf16[128,1536]{1,0:T(8,128)(2,1)}, bf16[128,1536]{1,0:T(8,128)(2,1)}) async-done(((bf16[128,1536]{1,0:T(8,128)(2,1)}, bf16[128,1536]{1,0:T(8,128)(2,1)}, bf16[128,1536]{1,0:T(8,128)(2,1)}, bf16[128,1536]{1,0:T(8,128)(2,1)}), (bf16[128,1536]{1,0:T(8,128)(2,1)}, bf16[128,1536]{1,0:T(8,128)(2,1)}, ...) | async-done | bytes 1572880
  (636 shorter events, 380.3 us)
Async XLA Ops:
  6.5 691.6 %copy-start = (bf16[288,1536]{1,0:T(8,128)(2,1)S(1)}, bf16[288,1536]{1,0:T(8,128)(2,1)}, u32[]{:S(2)}) copy-start(bf16[288,1536]{1,0:T(8,128)(2,1)} %param.43) | copy-start | bytes 2654212
  12.4 22.5 %all-to-all-start = ((bf16[4,8,1,1536]{3,0,2,1:T(4,128)(2,1)}), bf16[4,8,1,1536]{3,0,2,1:T(4,128)(2,1)S(1)}, u32[]{:S(2)}, u32[]{:S(2)}) async-start(bf16[4,8,1,1536]{3,0,2,1:T(4,128)(2,1)} %copy.313), calls=%async_computation | async-start | bytes 196608 | tf_op jit(solution)/shard_map/all_to_all | solution.py:139
  18.2 407.1 %all-gather.11.cloned.1.call-start = ((), (), s32[]{:S(2)}) async-start(), calls=%async_computation.5 | async-start | bytes 13369344 | tf_op jit(solution)/shard_map/all_gather | solution.py:14
  63.7 409.4 %all-gather.5.cloned.1.call-start = ((), (), s32[]{:S(2)}) async-start(), calls=%async_computation.2 | async-start | bytes 13369344 | tf_op jit(solution)/shard_map/all_gather | solution.py:14
  92.9 429.2 %all-gather.7.cloned.1.call-start = ((), (), s32[]{:S(2)}) async-start(), calls=%async_computation.3 | async-start | bytes 13369344 | tf_op jit(solution)/shard_map/all_gather | solution.py:14
  120.4 488.5 %all-gather.9.cloned.1.call-start = ((), (), s32[]{:S(2)}) async-start(), calls=%async_computation.4 | async-start | bytes 13369344 | tf_op jit(solution)/shard_map/all_gather | solution.py:14
  167.8 246.9 %copy-start.21 = (bf16[128,4,256]{2,1,0:T(4,128)(2,1)}, bf16[128,4,256]{2,1,0:T(4,128)(2,1)S(1)}, u32[]{:S(2)}) copy-start(bf16[128,4,256]{2,1,0:T(4,128)(2,1)S(1)} %scatter.15) | copy-start | bytes 786436
  190.5 226.4 %copy-start.20 = (bf16[128,4,256]{2,1,0:T(4,128)(2,1)}, bf16[128,4,256]{2,1,0:T(4,128)(2,1)S(1)}, u32[]{:S(2)}) copy-start(bf16[128,4,256]{2,1,0:T(4,128)(2,1)S(1)} %scatter.16) | copy-start | bytes 786436
  248.7 169.2 %copy-start.27 = (bf16[128,4,256]{2,1,0:T(4,128)(2,1)}, bf16[128,4,256]{2,1,0:T(4,128)(2,1)S(1)}, u32[]{:S(2)}) copy-start(bf16[128,4,256]{2,1,0:T(4,128)(2,1)S(1)} %scatter.19) | copy-start | bytes 786436
  248.8 171.7 %copy-start.11 = (f32[8,1152,8,12]{1,3,2,0:T(8,128)S(1)}, f32[8,1152,8,12]{1,3,2,0:T(8,128)}, u32[]{:S(2)}) copy-start(f32[8,1152,8,12]{1,3,2,0:T(8,128)} %copy-done.10) | copy-start | bytes 10616836
  312.0 107.6 %copy-start.18 = (f32[16,16,8,12]{1,2,3,0:T(8,128)}, f32[16,16,8,12]{1,2,3,0:T(8,128)S(1)}, u32[]{:S(2)}) copy-start(f32[16,16,8,12]{1,2,3,0:T(8,128)S(1)} %all_gather.73) | copy-start | bytes 294916
  334.6 85.0 %copy-start.19 = (f32[16,16,8,12]{1,2,3,0:T(8,128)}, f32[16,16,8,12]{1,2,3,0:T(8,128)S(1)}, u32[]{:S(2)}) copy-start(f32[16,16,8,12]{1,2,3,0:T(8,128)S(1)} %all_gather.74) | copy-start | bytes 294916
  356.3 62.5 %copy-start.16 = (f32[16,16,8,12]{1,2,3,0:T(8,128)}, f32[16,16,8,12]{1,2,3,0:T(8,128)S(1)}, u32[]{:S(2)}) copy-start(f32[16,16,8,12]{1,2,3,0:T(8,128)S(1)} %all_gather.79) | copy-start | bytes 294916
  424.4 490.5 %all-reduce.7.cloned.1.call-start = ((), (), s32[]{:S(2)}) async-start(), calls=%async_computation.6 | async-start | bytes 3145728
  475.2 46.6 %copy-start.40 = (f32[8,1,12]{2,1,0:T(1,128)S(1)}, f32[8,1,12]{2,1,0:T(1,128)}, u32[]{:S(2)}) copy-start(f32[8,1,12]{2,1,0:T(1,128)} %fusion.132) | copy-start | bytes 1156
  524.5 73.9 %copy-start.34 = (f32[8,12]{1,0:T(8,128)S(1)}, f32[8,12]{1,0:T(8,128)}, u32[]{:S(2)}) copy-start(f32[8,12]{1,0:T(8,128)} %copy-done.33) | copy-start | bytes 1156
  524.5 73.9 %copy-start.35 = (f32[8,12]{1,0:T(8,128)S(1)}, f32[8,12]{1,0:T(8,128)}, u32[]{:S(2)}) copy-start(f32[8,12]{1,0:T(8,128)} %convert_reduce_fusion.6) | copy-start | bytes 1156
  608.8 52.2 %copy-start.23 = (f32[8,1536]{1,0:T(8,128)}, f32[8,1536]{1,0:T(8,128)S(1)}, u32[]{:S(2)}) copy-start(f32[8,1536]{1,0:T(8,128)S(1)} %get-tuple-element.1037) | copy-start | bytes 147460
  610.2 46.5 %copy-start.30 = (f32[8,12]{1,0:T(8,128)S(1)}, f32[8,12]{1,0:T(8,128)}, u32[]{:S(2)}) copy-start(f32[8,12]{1,0:T(8,128)} %copy-done.29) | copy-start | bytes 1156
  610.2 46.5 %copy-start.31 = (f32[8,12]{1,0:T(8,128)S(1)}, f32[8,12]{1,0:T(8,128)}, u32[]{:S(2)}) copy-start(f32[8,12]{1,0:T(8,128)} %convert_reduce_fusion.5) | copy-start | bytes 1156
  661.8 58.5 %copy-start.3 = (bf16[1536,288]{0,1:T(8,128)(2,1)S(1)}, bf16[1536,288]{0,1:T(8,128)(2,1)}, u32[]{:S(2)}) copy-start(bf16[1536,288]{0,1:T(8,128)(2,1)} %param.41) | copy-start | bytes 2654212
  720.7 194.2 %copy-start.24 = (f32[8,1536]{1,0:T(8,128)S(1)}, f32[8,1536]{1,0:T(8,128)}, u32[]{:S(2)}) copy-start(f32[8,1536]{1,0:T(8,128)} %copy-done.23) | copy-start | bytes 147460
  720.7 195.0 %copy-start.26 = (f32[8,1536]{1,0:T(8,128)S(1)}, f32[8,1536]{1,0:T(8,128)}, u32[]{:S(2)}) copy-start(f32[8,1536]{1,0:T(8,128)} %copy-done.25) | copy-start | bytes 147460
  919.3 11.4 %all-to-all-start.1 = ((bf16[4,8,1,1536]{3,0,2,1:T(4,128)(2,1)}), bf16[4,8,1,1536]{3,0,2,1:T(4,128)(2,1)S(1)}, u32[]{:S(2)}, u32[]{:S(2)}) async-start(bf16[4,8,1,1536]{3,0,2,1:T(4,128)(2,1)} %bitcast.140), calls=%async_computation.1 | async-start | bytes 196608 | tf_op jit(solution)/shard_map/all_to_all | solution.py:208
  (33 other events, 423.8 us)
Sparse Core Ops, SparseCore 0:
  63.8 97.4 all-gather.10
  163.5 91.9 all-gather.4
  257.7 102.1 all-gather.6
  424.5 152.7 all-gather.8
  742.9 172.0 all-reduce.6
where the time goes:
time: 955 us; the launch traced here: 939 us
  blocking collectives  387 us (41%)
  waiting for transfers between devices  176 us (18%)
  other arithmetic  146 us (15%)
  local copies, waits for them, and re-layouts  144 us (15%)
  matrix products  56.8 us (6%)
  between operations  15.5 us (2%)
  starting transfers between devices  12.6 us (1%)
    unnamed x6, waiting for transfers between devices  171 us
    all_gather x8, blocking collectives, merged_2(): everything = jax.tree.map(lambda part: lax.all_gather(part, axis), array)  165 us
    all_gather x4, blocking collectives, on_device(): lax.all_gather(query, 'kv', axis=0, tiled=True)  79.3 us
    all_gather x4, blocking collectives, on_device(): lax.all_gather(fresh, 'kv', axis=0, tiled=True)  73.6 us
    dynamic_slice x60, local copies, waits for them, and re-layouts, turn(): return combine(so_far, jax.tree.map(lambda part: part[k], everything))  71.7 us
    add x60, other arithmetic, join_parts(): first[2] * scale_first[..., None] + second[2] * scale_second[..., None]  70.3 us
    all_gather x4, blocking collectives, on_device(): lax.all_gather(rms_round(residual, norm_mlp), 'kv', axis=0, tiled=True)  68.5 us
    add x64, other arithmetic, join_parts(): totals = first[1] * scale_first + second[1] * scale_second  53.3 us
  transfers between devices with their start and end apart: 7, of which 2 were waited for; matrix products, arithmetic and copies ran while one was open for 27% of the time, Pallas kernels for 0%

commit v1 on v0

--- a/solution.py
+++ b/solution.py
@@ -8,6 +8,14 @@
 BEAMS = 8
 EPSILON = 1e-06
 NEGATIVE = -1e30
+
+
+def balance_cells_over_axis(original):
+    queue = []
+    for _ in range(lax.axis_size("kv")):
+        queue.append(original)
+    known = jnp.concatenate(queue, axis=0)
+    return lax.all_to_all(known, "kv", 0, 0, tiled=True)
 
 
 def merged_2(array, axis, combine):
@@ -193,10 +201,7 @@
             + jnp.dot(attended, w_out, preferred_element_type=jnp.float32)
         ).astype(jnp.bfloat16)
         terms = feed_forward(
-            lax.all_gather(rms_round(residual, norm_mlp), "kv", axis=0, tiled=True),
-            w_gate,
-            w_up,
-            w_down,
+            balance_cells_over_axis(rms_round(residual, norm_mlp)), w_gate, w_up, w_down
         )
         summed = lax.psum_scatter(
             terms.astype(jnp.bfloat16), "kv", scatter_dimension=0, tiled=True

time: 955 us -> 933 us (0.977)
  blocking collectives: 387 us -> 329 us
  local copies, waits for them, and re-layouts: 144 us -> 164 us
  starting transfers between devices: 12.6 us -> 30.1 us
    all_gather x4 -> x0, blocking collectives: 68.5 us -> none  [on_device(): lax.all_gather(rms_round(residual, norm_mlp), 'kv', axis=0, tiled=True)]
    unnamed x101 -> x159, local copies, waits for them, and re-layouts: 9.75 us -> 28.3 us
    unnamed x6, waiting for transfers between devices: 171 us -> 153 us
    all_to_all x0 -> x4, starting transfers between devices: none -> 17.7 us  [balance_cells_over_axis(): return lax.all_to_all(known, 'kv', 0, 0, tiled=True)]
    all_gather x4, blocking collectives: 79.3 us -> 91.5 us  [on_device(): lax.all_gather(query, 'kv', axis=0, tiled=True)]
    all_to_all x0 -> x4, waiting for transfers between devices: none -> 12.1 us  [balance_cells_over_axis(): return lax.all_to_all(known, 'kv', 0, 0, tiled=True)]
  transfers between devices with their start and end apart: 7 -> 11, of which waited for: 2 -> 5; matrix products, arithmetic and copies ran while one was open for 27% -> 31% of each run, Pallas kernels for 0% -> 0%
where the time goes in v1:
time: 933 us; the launch traced here: 917 us
  blocking collectives  329 us (35%)
  waiting for transfers between devices  170 us (18%)
  local copies, waits for them, and re-layouts  164 us (18%)
  other arithmetic  146 us (16%)
  matrix products  59.9 us (6%)
  starting transfers between devices  30.1 us (3%)
  between operations  15.8 us (2%)
    all_gather x8, blocking collectives, merged_2(): everything = jax.tree.map(lambda part: lax.all_gather(part, axis), array)  165 us
    unnamed x6, waiting for transfers between devices  153 us
    all_gather x4, blocking collectives, on_device(): lax.all_gather(query, 'kv', axis=0, tiled=True)  91.5 us
    all_gather x4, blocking collectives, on_device(): lax.all_gather(fresh, 'kv', axis=0, tiled=True)  72.8 us
    dynamic_slice x60, local copies, waits for them, and re-layouts, turn(): return combine(so_far, jax.tree.map(lambda part: part[k], everything))  71.8 us
    add x60, other arithmetic, join_parts(): first[2] * scale_first[..., None] + second[2] * scale_second[..., None]  69.9 us
    add x64, other arithmetic, join_parts(): totals = first[1] * scale_first + second[1] * scale_second  53.3 us
    unnamed x159, local copies, waits for them, and re-layouts  28.3 us
  transfers between devices with their start and end apart: 11, of which 5 were waited for; matrix products, arithmetic and copies ran while one was open for 31% of the time, Pallas kernels for 0%

profile of v1, /device:TPU:1, one launch (start us, length us, event | category | flops | bytes accessed | tf_op | source)
XLA Modules:
  0.0 916.5 jit_solution(632328622568032233)
XLA Ops:
  27.1 7.8 gather_fusion.4
  39.2 20.2 %all_gather.75 = bf16[128,1536]{1,0:T(8,128)(2,1)S(1)} all-gather(bf16[8,1536]{1,0:T(8,128)(2,1)S(1)} %convolution_convert_fusion.4), channel_id=1, replica_groups=mesh['req'=8,'kv'=16] {'kv'}, dimensions={0}, use_global_device_ids=true | all-gather | bytes 417792 | tf_op jit(solution)/shard_map/all_gather | solution.py:173
  67.3 19.5 %all_gather.60 = bf16[128,1536]{1,0:T(8,128)(2,1)S(1)} all-gather(bf16[8,1536]{1,0:T(8,128)(2,1)S(1)} %convolution_convert_fusion.7), channel_id=1, replica_groups=mesh['req'=8,'kv'=16] {'kv'}, dimensions={0}, use_global_device_ids=true | all-gather | bytes 417792 | tf_op jit(solution)/shard_map/all_gather | solution.py:173
  96.5 30.3 %all_gather.65 = bf16[128,1536]{1,0:T(8,128)(2,1)S(1)} all-gather(bf16[8,1536]{1,0:T(8,128)(2,1)S(1)} %convolution_convert_fusion.6), channel_id=1, replica_groups=mesh['req'=8,'kv'=16] {'kv'}, dimensions={0}, use_global_device_ids=true | all-gather | bytes 417792 | tf_op jit(solution)/shard_map/all_gather | solution.py:173
  138.3 20.3 %all_gather.64 = bf16[128,256]{1,0:T(8,128)(2,1)S(1)} all-gather(bf16[8,256]{1,0:T(8,128)(2,1)S(1)} %convolution_convert_fusion.11), channel_id=1, replica_groups=mesh['req'=8,'kv'=16] {'kv'}, dimensions={0}, use_global_device_ids=true | all-gather | bytes 69632 | tf_op jit(solution)/shard_map/all_gather | solution.py:174
  161.5 15.6 %all_gather.69 = bf16[128,256]{1,0:T(8,128)(2,1)S(1)} all-gather(bf16[8,256]{1,0:T(8,128)(2,1)S(1)} %convolution_convert_fusion.10), channel_id=1, replica_groups=mesh['req'=8,'kv'=16] {'kv'}, dimensions={0}, use_global_device_ids=true | all-gather | bytes 69632 | tf_op jit(solution)/shard_map/all_gather | solution.py:174
  180.1 19.2 %all_gather.74 = bf16[128,256]{1,0:T(8,128)(2,1)S(1)} all-gather(bf16[8,256]{1,0:T(8,128)(2,1)S(1)} %convolution_convert_fusion.9), channel_id=1, replica_groups=mesh['req'=8,'kv'=16] {'kv'}, dimensions={0}, use_global_device_ids=true | all-gather | bytes 69632 | tf_op jit(solution)/shard_map/all_gather | solution.py:174
  202.2 17.7 %all_gather.79 = bf16[128,256]{1,0:T(8,128)(2,1)S(1)} all-gather(bf16[8,256]{1,0:T(8,128)(2,1)S(1)} %convolution_convert_fusion.8), channel_id=1, replica_groups=mesh['req'=8,'kv'=16] {'kv'}, dimensions={0}, use_global_device_ids=true | all-gather | bytes 69632 | tf_op jit(solution)/shard_map/all_gather | solution.py:174
  230.5 21.5 %all_gather.70 = bf16[128,1536]{1,0:T(8,128)(2,1)S(1)} all-gather(bf16[8,1536]{1,0:T(8,128)(2,1)S(1)} %convolution_convert_fusion.5), channel_id=1, replica_groups=mesh['req'=8,'kv'=16] {'kv'}, dimensions={0}, use_global_device_ids=true | all-gather | bytes 417792 | tf_op jit(solution)/shard_map/all_gather | solution.py:173
  260.0 21.0 %all_gather.76 = f32[16,16,8,12]{1,2,3,0:T(8,128)} all-gather(f32[1,16,8,12]{1,2,3,0:T(8,128)S(1)} %copy.375), channel_id=1, replica_groups=mesh['req'=8,'kv'=16] {'kv'}, dimensions={0}, use_global_device_ids=true | all-gather | bytes 104448 | tf_op jit(solution)/shard_map/all_gather | solution.py:22
  281.0 22.5 %all_gather.77 = f32[16,16,8,12]{1,2,3,0:T(8,128)} all-gather(f32[1,16,8,12]{1,2,3,0:T(8,128)S(1)} %copy.378), channel_id=1, replica_groups=mesh['req'=8,'kv'=16] {'kv'}, dimensions={0}, use_global_device_ids=true | all-gather | bytes 104448 | tf_op jit(solution)/shard_map/all_gather | solution.py:22
  303.5 21.2 %all_gather.61 = f32[16,16,8,12]{1,2,3,0:T(8,128)S(1)} all-gather(f32[1,16,8,12]{1,2,3,0:T(8,128)S(1)} %copy.320), channel_id=1, replica_groups=mesh['req'=8,'kv'=16] {'kv'}, dimensions={0}, use_global_device_ids=true | all-gather | bytes 104448 | tf_op jit(solution)/shard_map/all_gather | solution.py:22
  324.7 23.0 %all_gather.62 = f32[16,16,8,12]{1,2,3,0:T(8,128)S(1)} all-gather(f32[1,16,8,12]{1,2,3,0:T(8,128)S(1)} %copy.323), channel_id=1, replica_groups=mesh['req'=8,'kv'=16] {'kv'}, dimensions={0}, use_global_device_ids=true | all-gather | bytes 104448 | tf_op jit(solution)/shard_map/all_gather | solution.py:22
  347.7 18.1 %all_gather.66 = f32[16,16,8,12]{1,2,3,0:T(8,128)S(1)} all-gather(f32[1,16,8,12]{1,2,3,0:T(8,128)S(1)} %copy.341), channel_id=1, replica_groups=mesh['req'=8,'kv'=16] {'kv'}, dimensions={0}, use_global_device_ids=true | all-gather | bytes 104448 | tf_op jit(solution)/shard_map/all_gather | solution.py:22
  365.8 19.6 %all_gather.67 = f32[16,16,8,12]{1,2,3,0:T(8,128)S(1)} all-gather(f32[1,16,8,12]{1,2,3,0:T(8,128)S(1)} %copy.344), channel_id=1, replica_groups=mesh['req'=8,'kv'=16] {'kv'}, dimensions={0}, use_global_device_ids=true | all-gather | bytes 104448 | tf_op jit(solution)/shard_map/all_gather | solution.py:22
  385.4 19.1 %all_gather.71 = f32[16,16,8,12]{1,2,3,0:T(8,128)} all-gather(f32[1,16,8,12]{1,2,3,0:T(8,128)S(1)} %copy.358), channel_id=1, replica_groups=mesh['req'=8,'kv'=16] {'kv'}, dimensions={0}, use_global_device_ids=true | all-gather | bytes 104448 | tf_op jit(solution)/shard_map/all_gather | solution.py:22
  404.5 20.1 %all_gather.72 = f32[16,16,8,12]{1,2,3,0:T(8,128)} all-gather(f32[1,16,8,12]{1,2,3,0:T(8,128)S(1)} %copy.361), channel_id=1, replica_groups=mesh['req'=8,'kv'=16] {'kv'}, dimensions={0}, use_global_device_ids=true | all-gather | bytes 104448 | tf_op jit(solution)/shard_map/all_gather | solution.py:22
  436.9 46.2 %while.83 = (s32[]{:T(128)}, f32[16,8,12]{0,1,2:T(8,128)S(1)}, f32[16,8,12]{0,1,2:T(8,128)S(1)}, f32[16,8,12,128]{3,2,1,0:T(8,128)S(1)}, f32[16,16,8,12]{1,2,3,0...) while((s32[]{:T(128)}, f32[16,8,12]{0,1,2:T(8,128)S(1)}, ...), condition=%wide.region_32.33_spmd, body=%wide.region_31.32_spmd.sunk | while | flops 599045 | bytes 4018327 | solution.py:28
  485.4 46.3 %while.80 = (s32[]{:T(128)}, f32[16,8,12]{0,1,2:T(8,128)S(1)}, f32[16,8,12]{0,1,2:T(8,128)S(1)}, f32[16,8,12,128]{3,2,1,0:T(8,128)S(1)}, f32[16,16,8,12]{1,2,3,0...) while((s32[]{:T(128)}, f32[16,8,12]{0,1,2:T(8,128)S(1)}, ...), condition=%wide.region_7.8_spmd, body=%wide.region_6.7_spmd.sunk | while | flops 599045 | bytes 4018327 | solution.py:28
  535.1 73.3 %while.81 = (s32[]{:T(128)}, f32[16,8,12]{0,1,2:T(8,128)S(1)}, f32[16,8,12]{0,1,2:T(8,128)S(1)}, f32[16,8,12,128]{3,2,1,0:T(8,128)}, f32[16,16,8,12]{1,2,3,0:T(8...) while((s32[]{:T(128)}, f32[16,8,12]{0,1,2:T(8,128)S(1)}, ...), condition=%wide.region_14.15_spmd, body=%wide.region_13.14_spmd.sunk | while | flops 599045 | bytes 4018327 | solution.py:28
  622.3 46.2 %while.82 = (s32[]{:T(128)}, f32[16,8,12]{0,1,2:T(8,128)S(1)}, f32[16,8,12]{0,1,2:T(8,128)S(1)}, f32[16,8,12,128]{3,2,1,0:T(8,128)S(1)}, f32[16,16,8,12]{1,2,3,0...) while((s32[]{:T(128)}, f32[16,8,12]{0,1,2:T(8,128)S(1)}, ...), condition=%wide.region_23.24_spmd, body=%wide.region_22.23_spmd.sunk | while | flops 599045 | bytes 4018327 | solution.py:28
  698.5 6.7 all-to-all-start.3
  739.6 152.9 %all-reduce.7.cloned.1.call-done = (bf16[128,1536]{1,0:T(8,128)(2,1)}, bf16[128,1536]{1,0:T(8,128)(2,1)}, bf16[128,1536]{1,0:T(8,128)(2,1)}, bf16[128,1536]{1,0:T(8,128)(2,1)}) async-done(((bf16[128,1536]{1,0:T(8,128)(2,1)}, bf16[128,1536]{1,0:T(8,128)(2,1)}, bf16[128,1536]{1,0:T(8,128)(2,1)}, bf16[128,1536]{1,0:T(8,128)(2,1)}), (bf16[128,1536]{1,0:T(8,128)(2,1)}, bf16[128,1536]{1,0:T(8,128)(2,1)}, ...) | async-done | bytes 1572880
  896.9 6.5 all-to-all-start.5
  (702 shorter events, 396.2 us)
Async XLA Ops:
  6.5 699.7 %copy-start = (bf16[288,1536]{1,0:T(8,128)(2,1)S(1)}, bf16[288,1536]{1,0:T(8,128)(2,1)}, u32[]{:S(2)}) copy-start(bf16[288,1536]{1,0:T(8,128)(2,1)} %param.43) | copy-start | bytes 2654212
  12.4 22.6 %all-to-all-start = ((bf16[4,8,1,1536]{3,0,2,1:T(4,128)(2,1)}), bf16[4,8,1,1536]{3,0,2,1:T(4,128)(2,1)S(1)}, u32[]{:S(2)}, u32[]{:S(2)}) async-start(bf16[4,8,1,1536]{3,0,2,1:T(4,128)(2,1)} %copy.313), calls=%async_computation | async-start | bytes 196608 | tf_op jit(solution)/shard_map/all_to_all | solution.py:147
  18.2 417.3 %all-gather.11.cloned.1.call-start = ((), (), s32[]{:S(2)}) async-start(), calls=%async_computation.9 | async-start | bytes 13369344 | tf_op jit(solution)/shard_map/all_gather | solution.py:22
  63.9 419.5 %all-gather.5.cloned.1.call-start = ((), (), s32[]{:S(2)}) async-start(), calls=%async_computation.6 | async-start | bytes 13369344 | tf_op jit(solution)/shard_map/all_gather | solution.py:22
  93.1 439.3 %all-gather.7.cloned.1.call-start = ((), (), s32[]{:S(2)}) async-start(), calls=%async_computation.7 | async-start | bytes 13369344 | tf_op jit(solution)/shard_map/all_gather | solution.py:22
  133.1 487.8 %all-gather.9.cloned.1.call-start = ((), (), s32[]{:S(2)}) async-start(), calls=%async_computation.8 | async-start | bytes 13369344 | tf_op jit(solution)/shard_map/all_gather | solution.py:22
  178.9 246.2 %copy-start.20 = (bf16[128,4,256]{2,1,0:T(4,128)(2,1)}, bf16[128,4,256]{2,1,0:T(4,128)(2,1)S(1)}, u32[]{:S(2)}) copy-start(bf16[128,4,256]{2,1,0:T(4,128)(2,1)S(1)} %scatter.15) | copy-start | bytes 786436
  201.1 226.3 %copy-start.19 = (bf16[128,4,256]{2,1,0:T(4,128)(2,1)}, bf16[128,4,256]{2,1,0:T(4,128)(2,1)S(1)}, u32[]{:S(2)}) copy-start(bf16[128,4,256]{2,1,0:T(4,128)(2,1)S(1)} %scatter.16) | copy-start | bytes 786436
  260.0 168.4 %copy-start.29 = (bf16[128,4,256]{2,1,0:T(4,128)(2,1)}, bf16[128,4,256]{2,1,0:T(4,128)(2,1)S(1)}, u32[]{:S(2)}) copy-start(bf16[128,4,256]{2,1,0:T(4,128)(2,1)S(1)} %scatter.19) | copy-start | bytes 786436
  260.0 170.9 %copy-start.10 = (f32[8,1152,8,12]{1,3,2,0:T(8,128)S(1)}, f32[8,1152,8,12]{1,3,2,0:T(8,128)}, u32[]{:S(2)}) copy-start(f32[8,1152,8,12]{1,3,2,0:T(8,128)} %copy-done.9) | copy-start | bytes 10616836
  324.7 105.3 %copy-start.17 = (f32[16,16,8,12]{1,2,3,0:T(8,128)}, f32[16,16,8,12]{1,2,3,0:T(8,128)S(1)}, u32[]{:S(2)}) copy-start(f32[16,16,8,12]{1,2,3,0:T(8,128)S(1)} %all_gather.61) | copy-start | bytes 294916
  347.7 82.4 %copy-start.18 = (f32[16,16,8,12]{1,2,3,0:T(8,128)}, f32[16,16,8,12]{1,2,3,0:T(8,128)S(1)}, u32[]{:S(2)}) copy-start(f32[16,16,8,12]{1,2,3,0:T(8,128)S(1)} %all_gather.62) | copy-start | bytes 294916
  535.1 73.6 %copy-start.35 = (f32[8,12]{1,0:T(8,128)S(1)}, f32[8,12]{1,0:T(8,128)}, u32[]{:S(2)}) copy-start(f32[8,12]{1,0:T(8,128)} %copy-done.34) | copy-start | bytes 1156
  535.1 73.6 %copy-start.36 = (f32[8,12]{1,0:T(8,128)S(1)}, f32[8,12]{1,0:T(8,128)}, u32[]{:S(2)}) copy-start(f32[8,12]{1,0:T(8,128)} %convert_reduce_fusion.6) | copy-start | bytes 1156
  675.5 22.2 %all-to-all-start.4 = ((bf16[16,8,1536]{2,1,0:T(8,128)(2,1)}), bf16[16,8,1536]{2,1,0:T(8,128)(2,1)S(1)}, u32[]{:S(2)}, u32[]{:S(2)}) async-start(bf16[16,8,1536]{2,1,0:T(8,128)(2,1)} %bitcast.641), calls=%async_computation.4 | async-start | bytes 786432 | tf_op jit(solution)/shard_map/all_to_all | solution.py:18
  698.5 14.6 %all-to-all-start.3 = ((bf16[16,8,1536]{2,1,0:T(8,128)(2,1)}), bf16[16,8,1536]{2,1,0:T(8,128)(2,1)S(1)}, u32[]{:S(2)}, u32[]{:S(2)}) async-start(bf16[16,8,1536]{2,1,0:T(8,128)(2,1)} %bitcast.640), calls=%async_computation.3 | async-start | bytes 786432 | tf_op jit(solution)/shard_map/all_to_all | solution.py:18
  713.1 11.5 %all-to-all-start.2 = ((bf16[16,8,1536]{2,1,0:T(8,128)(2,1)}), bf16[16,8,1536]{2,1,0:T(8,128)(2,1)S(1)}, u32[]{:S(2)}, u32[]{:S(2)}) async-start(bf16[16,8,1536]{2,1,0:T(8,128)(2,1)} %bitcast.639), calls=%async_computation.2 | async-start | bytes 786432 | tf_op jit(solution)/shard_map/all_to_all | solution.py:18
  724.6 11.5 %all-to-all-start.1 = ((bf16[16,8,1536]{2,1,0:T(8,128)(2,1)}), bf16[16,8,1536]{2,1,0:T(8,128)(2,1)S(1)}, u32[]{:S(2)}, u32[]{:S(2)}) async-start(bf16[16,8,1536]{2,1,0:T(8,128)(2,1)} %bitcast.638), calls=%async_computation.1 | async-start | bytes 786432 | tf_op jit(solution)/shard_map/all_to_all | solution.py:18
  728.2 165.8 %copy-start.25 = (f32[8,1536]{1,0:T(8,128)S(1)}, f32[8,1536]{1,0:T(8,128)}, u32[]{:S(2)}) copy-start(f32[8,1536]{1,0:T(8,128)} %get-tuple-element.1039) | copy-start | bytes 147460
  728.2 164.3 %all-reduce.7.cloned.1.call-start = ((), (), s32[]{:S(2)}) async-start(), calls=%async_computation.10 | async-start | bytes 3145728
  729.4 165.4 %copy-start.24 = (f32[8,1536]{1,0:T(8,128)S(1)}, f32[8,1536]{1,0:T(8,128)}, u32[]{:S(2)}) copy-start(f32[8,1536]{1,0:T(8,128)} %get-tuple-element.1033) | copy-start | bytes 147460
  732.2 160.3 %copy-start.26 = (f32[8,1536]{1,0:T(8,128)S(1)}, f32[8,1536]{1,0:T(8,128)}, u32[]{:S(2)}) copy-start(f32[8,1536]{1,0:T(8,128)} %get-tuple-element.1047) | copy-start | bytes 147460
  732.2 161.1 %copy-start.28 = (f32[8,1536]{1,0:T(8,128)S(1)}, f32[8,1536]{1,0:T(8,128)}, u32[]{:S(2)}) copy-start(f32[8,1536]{1,0:T(8,128)} %copy-done.27) | copy-start | bytes 147460
  896.9 11.4 %all-to-all-start.5 = ((bf16[4,8,1,1536]{3,0,2,1:T(4,128)(2,1)}), bf16[4,8,1,1536]{3,0,2,1:T(4,128)(2,1)S(1)}, u32[]{:S(2)}, u32[]{:S(2)}) async-start(bf16[4,8,1,1536]{3,0,2,1:T(4,128)(2,1)} %bitcast.148), calls=%async_computation.5 | async-start | bytes 196608 | tf_op jit(solution)/shard_map/all_to_all | solution.py:213
  (38 other events, 546.8 us)
Sparse Core Ops, SparseCore 0:
  64.0 97.7 all-gather.10
  164.0 91.4 all-gather.4
  257.8 100.7 all-gather.6
  435.0 151.9 all-gather.8
  738.5 153.9 all-reduce.6
